TPU v7x, 256 devices: a whole 4x4x8 slice. The times are simulated.
256 devices in a mesh: row: 8 (over x, core), col: 32 (over y, z).
Axes of the slice: x: 4, y: 4, z: 8, core: 2. Of those that a mesh axis runs over, the one named last changes fastest.
Arguments:
- tokens: bfloat16 [1024, 6144], P('col', 'row'), may hold values from -6 to 6
- w_up: bfloat16 [6144, 24576], P('row', 'col'), may hold values from -0.078125 to 0.078125
- w_down: bfloat16 [24576, 6144], P('col', 'row'), may hold values from -0.0390625 to 0.0390625
- expert_in: bfloat16 [6144, 8192], P(None, 'col'), may hold values from -0.078125 to 0.078125
- expert_out: bfloat16 [8192, 6144], P('col'), may hold values from -0.125 to 0.125
- expert_ids: int32 [1024, 2], P('col'), may hold values from 0 to 3, as said below
- route_weights: bfloat16 [1024, 2], P('col'), may hold values from 0.25 to 1
- out_grad: bfloat16 [1024, 6144], P('col', 'row'), may hold values from -6 to 6
Outputs:
- layer_out: bfloat16 [1024, 6144], P('col', 'row')
- tokens_grad: bfloat16 [1024, 6144], P('col', 'row')
- up_grad: bfloat16 [6144, 24576], P('row', 'col')
- down_grad: bfloat16 [24576, 6144], P('col', 'row')
- expert_in_grad: bfloat16 [6144, 8192], P('row', 'col')
- expert_out_grad: bfloat16 [8192, 6144], P('col', 'row')
Inputs may be any that keep to these rules, and one draw needn't show every extreme that they name: `expert_ids`: the two experts of a token differ. In every aligned block of 4 tokens no expert is named by more than 3 of the block's pairs; one expert is named by exactly 3 pairs, the same expert in all blocks whose index leaves the same remainder modulo 32 // 4; the other experts' counts in a block differ by at most one. Every expert is named somewhere.
All inputs are finite; a program needn't handle non-finite values.
Results may differ from a plain program's by a relative error of at most 0.025.
Values may be sent and summed in bfloat16 or wider, within the bound.
No kernel may reach another device: no remote copies, remote signals or barrier semaphores. Data moves between devices by JAX's collectives and lax.ppermute only.
A program may use at most 128 MiB of HBM per device.

v0:
```python
import jax
import jax.numpy as jnp
from jax import lax
from jax.sharding import PartitionSpec as P

EXPERTS = 4
gelu_scale = 0.7978845608028654
gelu_cubic = 0.044715


def gelu_tanh(value):
    return 0.5 * value * (1.0 + jnp.tanh(gelu_scale * (value + gelu_cubic * value * value * value)))


def gelu_slope(value):
    inner = jnp.tanh(gelu_scale * (value + gelu_cubic * value * value * value))
    return 0.5 * (1.0 + inner) + 0.5 * value * (1.0 - inner * inner) * gelu_scale * (
        1.0 + 3.0 * gelu_cubic * value * value
    )


def slot_ranks(pairs):
    count = pairs.shape[-1]
    positions = jnp.arange(count, dtype=jnp.int32)
    earlier = positions[:, None] > positions[None, :]
    matching = pairs[..., :, None] == pairs[..., None, :]
    return jnp.sum((matching & earlier).astype(jnp.int32), axis=-1)


def gather_rows(part, axis_name):
    count = lax.axis_size(axis_name)
    spread = jnp.broadcast_to(part[None], (count,) + part.shape)
    got = lax.all_to_all(spread, axis_name, 0, 0, tiled=True)
    return got.reshape((count * part.shape[0],) + part.shape[1:])


def scatter_sum(terms, axis_name):
    count = lax.axis_size(axis_name)
    blocks = terms.astype(jnp.bfloat16).reshape((count, terms.shape[0] // count) + terms.shape[1:])
    got = lax.all_to_all(blocks, axis_name, 0, 0, tiled=True)
    return got.astype(jnp.float32).sum(axis=0)


def scatter_sum_cols(terms, axis_name):
    count = lax.axis_size(axis_name)
    got = lax.all_to_all(terms.astype(jnp.bfloat16), axis_name, 1, 0, tiled=True)
    return (
        got.reshape((count, terms.shape[0], terms.shape[1] // count))
        .astype(jnp.float32)
        .sum(axis=0)
    )


def dense_exchange(payload, axis_name):
    shape = payload.shape
    flat = payload.reshape(shape[0], -1, 128)
    got = lax.all_to_all(flat, axis_name, 0, 0, tiled=True)
    return got.reshape(shape)


def swap_blocks(pair, count):
    arrays, tok, width = pair.shape
    block = tok // count
    parts = pair.reshape(arrays, count, block, width).transpose(1, 0, 2, 3)
    got = lax.all_to_all(parts.reshape(count, arrays * block, width), "row", 0, 0, tiled=True)
    got = got.reshape(count, arrays, block, width).transpose(1, 2, 0, 3)
    return got.reshape(arrays, block, count * width)


def unswap_blocks(pair, count):
    arrays, block, full = pair.shape
    width = full // count
    parts = pair.reshape(arrays, block, count, width).transpose(2, 0, 1, 3)
    got = lax.all_to_all(parts.reshape(count, arrays * block, width), "row", 0, 0, tiled=True)
    got = got.reshape(count, arrays, block, width).transpose(1, 0, 2, 3)
    return got.reshape(arrays, count * block, width)


def on_device(tokens, w_up, w_down, expert_in, expert_out, expert_ids, route_weights, out_grad):
    row_count = lax.axis_size("row")
    col_count = lax.axis_size("col")
    tok_col = tokens.shape[0]
    block_len = tok_col // row_count
    group_len = col_count // EXPERTS
    slot_cap = max(2, 3 * block_len // 4)
    model_width = expert_out.shape[1]
    my_row = lax.axis_index("row")
    own_grad = swap_blocks(out_grad[None], row_count)[0]
    ids_own = lax.dynamic_slice_in_dim(expert_ids, my_row * block_len, block_len, 0)
    weights_own = lax.dynamic_slice_in_dim(route_weights, my_row * block_len, block_len, 0)
    expert_range = jnp.arange(EXPERTS, dtype=jnp.int32)
    weight_table = jnp.sum(
        weights_own.astype(jnp.float32)[None, :, :]
        * (ids_own[None, :, :] == expert_range[:, None, None]).astype(jnp.float32),
        axis=2,
    )
    table_row = jnp.pad(
        weight_table.reshape(1, EXPERTS * block_len).astype(jnp.bfloat16),
        ((0, 0), (0, model_width - EXPERTS * block_len)),
    )
    grad_pack = jnp.concatenate([own_grad, table_row], axis=0)
    tokens_ready, grad_pack = lax.optimization_barrier((tokens, grad_pack))
    tok_panel = gather_rows(tokens_ready, "col")
    pack_all = lax.all_gather(grad_pack, "col", axis=0, tiled=False)
    my_expert = lax.axis_index("col") // group_len
    weights_recv = lax.dynamic_slice_in_dim(
        pack_all[:, block_len, : EXPERTS * block_len], my_expert * block_len, block_len, 1
    )
    grad_rows_in = (
        weights_recv.astype(jnp.float32)[:, :, None] * pack_all[:, :block_len].astype(jnp.float32)
    ).astype(jnp.bfloat16)
    up_terms = jnp.dot(tok_panel, w_up, preferred_element_type=jnp.float32)
    preact = scatter_sum(up_terms, "row")
    hidden_full = gather_rows(gelu_tanh(preact).astype(jnp.bfloat16), "row")
    rows_in = hidden_full
    down_terms, pack_all = lax.optimization_barrier(
        (jnp.dot(rows_in, w_down, preferred_element_type=jnp.float32), pack_all)
    )
    dense_term = scatter_sum(down_terms, "col")
    mixed_act = (tokens.astype(jnp.float32) + dense_term).astype(jnp.bfloat16)
    own_rows = swap_blocks(mixed_act[None], row_count)[0]
    scaled_flat = grad_rows_in.reshape(col_count * block_len, model_width)
    payload = jnp.broadcast_to(own_rows[None], (col_count,) + own_rows.shape)
    got = lax.all_to_all(payload, "col", 0, 0, tiled=True)
    got_flat = got.reshape(col_count * block_len, model_width)
    hid_units = expert_in.shape[1]
    e_pre = jnp.dot(got_flat, expert_in, preferred_element_type=jnp.float32).reshape(
        col_count, block_len, hid_units
    )
    g_dot = jnp.dot(scaled_flat, expert_out.T, preferred_element_type=jnp.float32).reshape(
        col_count, block_len, hid_units
    )
    e_hidden = gelu_tanh(e_pre).astype(jnp.bfloat16)
    e_dpre = (g_dot * gelu_slope(e_pre)).astype(jnp.bfloat16)
    blank = jnp.zeros_like(e_hidden)

    def at_rows(value, first):
        halves = [value, blank] if first else [blank, value]
        return jnp.concatenate(halves, axis=1).reshape(col_count * 2 * block_len, hid_units)

    back_flat = jnp.dot(
        at_rows(e_hidden, True), expert_out, preferred_element_type=jnp.float32
    ) + jnp.dot(at_rows(e_dpre, False), expert_in.T, preferred_element_type=jnp.float32)
    grad_in = jnp.dot(
        got_flat.T,
        e_dpre.reshape(col_count * block_len, hid_units),
        preferred_element_type=jnp.float32,
    )
    grad_out = jnp.dot(
        e_hidden.reshape(col_count * block_len, hid_units).T,
        scaled_flat,
        preferred_element_type=jnp.float32,
    )
    back = (
        lax.all_to_all(
            back_flat.astype(jnp.bfloat16)
            .reshape(col_count, 2 * block_len, row_count, model_width // row_count)
            .transpose(2, 0, 1, 3)
            .reshape(row_count * col_count, 2 * block_len, model_width // row_count),
            ("row", "col"),
            0,
            0,
            tiled=True,
        )
        .astype(jnp.float32)
        .reshape(row_count, col_count, 2 * block_len, model_width // row_count)
    )
    local_table = jnp.sum(
        route_weights.astype(jnp.float32)[:, None, :]
        * (expert_ids[:, None, :] == expert_range[None, :, None]).astype(jnp.float32),
        axis=2,
    )
    source_weights = jnp.repeat(
        local_table.reshape(row_count, block_len, EXPERTS).transpose(0, 2, 1), group_len, axis=1
    )
    moe_sum = jnp.sum(source_weights[:, :, :, None] * back[:, :, :block_len], axis=1)
    grad_sum = jnp.sum(back[:, :, block_len:], axis=1)
    layer_out = (mixed_act.astype(jnp.float32) + moe_sum.reshape(tok_col, -1)).astype(jnp.bfloat16)
    mixed_grad = (out_grad.astype(jnp.float32) + grad_sum.reshape(tok_col, -1)).astype(jnp.bfloat16)
    expert_in_grad = lax.psum_scatter(
        grad_in.astype(jnp.bfloat16).astype(jnp.float32), "row", scatter_dimension=0, tiled=True
    ).astype(jnp.bfloat16)
    expert_out_grad = lax.psum_scatter(
        grad_out.astype(jnp.bfloat16).astype(jnp.float32), "row", scatter_dimension=1, tiled=True
    ).astype(jnp.bfloat16)
    cot_panel = gather_rows(mixed_grad, "col")
    hgrad_terms = jnp.dot(cot_panel, w_down.T, preferred_element_type=jnp.float32)
    down_grad = jnp.dot(hidden_full.T, cot_panel, preferred_element_type=jnp.float32).astype(
        jnp.bfloat16
    )
    hidden_grad = scatter_sum(hgrad_terms, "row")
    dpre_full = gather_rows((hidden_grad * gelu_slope(preact)).astype(jnp.bfloat16), "row")
    up_grad = jnp.dot(tok_panel.T, dpre_full, preferred_element_type=jnp.float32).astype(
        jnp.bfloat16
    )
    rows_in = dpre_full
    input_term = scatter_sum(jnp.dot(rows_in, w_up.T, preferred_element_type=jnp.float32), "col")
    tokens_grad = (mixed_grad.astype(jnp.float32) + input_term).astype(jnp.bfloat16)
    return (layer_out, tokens_grad, up_grad, down_grad, expert_in_grad, expert_out_grad)


def solution(mesh):
    in_specs = (
        P("col", "row"),
        P("row", "col"),
        P("col", "row"),
        P(None, "col"),
        P("col", None),
        P("col", None),
        P("col", None),
        P("col", "row"),
    )
    out_specs = (
        P("col", "row"),
        P("col", "row"),
        P("row", "col"),
        P("col", "row"),
        P("row", "col"),
        P("col", "row"),
    )
    return jax.shard_map(
        on_device, mesh=mesh, in_specs=in_specs, out_specs=out_specs, check_vma=False
    )
```

profile of v0, /device:TPU:32, one launch (start us, length us, event | category | flops | bytes accessed | tf_op | source)
XLA Modules:
  0.0 489.2 jit_solution(7330491538299597089)
XLA Ops:
  7.2 1.6 reshape_transpose_reshape_broadcast_in_dim.6
  8.8 4.3 all-to-all-start
  13.1 0.7 constant_dynamic-slice_fusion.2
  13.8 0.7 fusion.33
  14.7 4.0 all-to-all-done
  18.6 0.7 fusion.32
  19.3 2.1 broadcast_in_dim.14
  21.4 11.4 %all-to-all-start.1 = ((bf16[32,32,768]{2,1,0:T(8,128)(2,1)}), bf16[32,32,768]{2,1,0:T(8,128)(2,1)}, u32[]{:S(2)}, u32[]{:S(2)}) async-start(bf16[32,32,768]{2,1,0:T(8,128)(2,1)} %broadcast_in_dim.14), calls=%async_computation.1 | async-start | bytes 3145728 | tf_op jit(solution)/shard_map/all_to_all | solution.py:33
  32.9 0.7 all-gather.4.cloned.1.call-update
  33.6 41.8 %all-to-all-done.1 = bf16[32,32,768]{2,1,0:T(8,128)(2,1)} async-done(((bf16[32,32,768]{2,1,0:T(8,128)(2,1)}), bf16[32,32,768]{2,1,0:T(8,128)(2,1)}, u32[]{:S(2)}, u32[]{:S(2)}) %all-to-all-start.1) | async-done | bytes 1572896 | tf_op jit(solution)/shard_map/all_to_all | solution.py:33
  75.4 3.1 convolution_convert_fusion.2
  78.5 24.0 %all_to_all.60 = bf16[8,128,768]{2,1,0:T(8,128)(2,1)S(1)} all-to-all(bf16[8,128,768]{2,1,0:T(8,128)(2,1)S(1)} %bitcast.88), channel_id=1, replica_groups=mesh['row'=8,'col'=32] {'row'}, dimensions={0} | all-to-all | bytes 3145728 | tf_op jit(solution)/shard_map/all_to_all | solution.py:40
  103.0 24.2 %all_to_all.61 = bf16[8,128,768]{2,1,0:T(8,128)(2,1)S(1)} all-to-all(bf16[8,128,768]{2,1,0:T(8,128)(2,1)S(1)} %broadcast_in_dim.15), channel_id=1, replica_groups=mesh['row'=8,'col'=32] {'row'}, dimensions={0} | all-to-all | bytes 3145728 | tf_op jit(solution)/shard_map/all_to_all | solution.py:33
  127.2 1.2 copy-done.4
  128.4 2.5 fusion.36
  130.9 45.4 %all_to_all.62 = bf16[32,32,768]{2,1,0:T(8,128)(2,1)S(1)} all-to-all(bf16[32,32,768]{2,1,0:T(8,128)(2,1)} %bitcast.87), channel_id=1, replica_groups=mesh['row'=8,'col'=32] {'col'}, dimensions={0} | all-to-all | bytes 3145728 | tf_op jit(solution)/shard_map/all_to_all | solution.py:40
  177.8 1.4 reshape_transpose_reshape_broadcast_in_dim.7
  179.2 8.8 %all_to_all.63 = bf16[8,4,768]{2,1,0:T(4,128)(2,1)S(1)} all-to-all(bf16[8,4,768]{2,1,0:T(4,128)(2,1)} %reshape_transpose_reshape_broadcast_in_dim.7), channel_id=1, replica_groups=mesh['row'=8,'col'=32] {'row'}, dimensions={0} | all-to-all | bytes 98304 | tf_op jit(solution)/shard_map/all_to_all | solution.py:65
  188.0 1.9 broadcast_in_dim.18
  189.8 4.9 %all-to-all-start.6 = ((bf16[32,4,6144]{2,1,0:T(4,128)(2,1)}), bf16[32,4,6144]{2,1,0:T(4,128)(2,1)}, u32[]{:S(2)}, u32[]{:S(2)}) async-start(bf16[32,4,6144]{2,1,0:T(4,128)(2,1)} %broadcast_in_dim.18), calls=%async_computation.6 | async-start | bytes 3145728 | tf_op jit(solution)/shard_map/all_to_all | solution.py:124
  195.0 0.9 slice.16
  196.6 3.7 slice.17
  200.3 33.5 %all-to-all-done.6 = bf16[32,4,6144]{2,1,0:T(4,128)(2,1)} async-done(((bf16[32,4,6144]{2,1,0:T(4,128)(2,1)}), bf16[32,4,6144]{2,1,0:T(4,128)(2,1)}, u32[]{:S(2)}, u32[]{:S(2)}) %all-to-all-start.6) | async-done | bytes 1572896 | tf_op jit(solution)/shard_map/all_to_all | solution.py:124
  233.9 3.4 multiply_convert_fusion.8
  238.0 4.1 fusion.4
  242.1 0.9 copy.69
  243.0 4.0 fusion.15
  247.6 1.0 fusion.31
  248.6 1.1 fusion
  249.7 1.8 copy.64
  251.5 7.0 %all-to-all-start.7 = ((bf16[256,8,768]{2,1,0:T(8,128)(2,1)}), bf16[256,8,768]{2,1,0:T(8,128)(2,1)S(1)}, u32[]{:S(2)}, u32[]{:S(2)}) async-start(bf16[256,8,768]{2,1,0:T(8,128)(2,1)} %bitcast.20), calls=%async_computation.7 | async-start | bytes 6291456 | tf_op jit(solution)/shard_map/all_to_all | solution.py:155
  258.6 5.5 %fusion.2 = f32[6144,256]{1,0:T(8,128)} fusion(bf16[32,4,256]{2,0,1:T(8,128)(2,1)} %copy-done.16, bf16[32,4,6144]{2,1,0:T(4,128)(2,1)} %all-to-all-done.6), kind=kOutput, calls=%fused_computation.5 | convolution fusion | flops 405798912 | bytes 7929856 | tf_op jit(solution)/shard_map/dot_general | solution.py:144
  265.4 0.8 reshape.142
  266.1 0.7 broadcast_bitcast_fusion
  266.8 67.2 %all-to-all-done.7 = bf16[256,8,768]{2,1,0:T(8,128)(2,1)S(1)} async-done(((bf16[256,8,768]{2,1,0:T(8,128)(2,1)}), bf16[256,8,768]{2,1,0:T(8,128)(2,1)S(1)}, u32[]{:S(2)}, u32[]{:S(2)}) %all-to-all-start.7) | async-done | bytes 3145760 | tf_op jit(solution)/shard_map/all_to_all | solution.py:155
  334.9 2.3 slice_reduce_fusion
  338.0 45.0 %all_to_all.64 = bf16[32,32,768]{2,1,0:T(8,128)(2,1)S(1)} all-to-all(bf16[32,32,768]{2,1,0:T(8,128)(2,1)S(1)} %broadcast_in_dim.19), channel_id=1, replica_groups=mesh['row'=8,'col'=32] {'col'}, dimensions={0} | all-to-all | bytes 3145728 | tf_op jit(solution)/shard_map/all_to_all | solution.py:33
  383.0 1.4 convolution_convert_fusion.1
  384.4 24.4 %all_to_all.65 = bf16[8,128,768]{2,1,0:T(8,128)(2,1)S(1)} all-to-all(bf16[8,128,768]{2,1,0:T(8,128)(2,1)S(1)} %bitcast.89), channel_id=1, replica_groups=mesh['row'=8,'col'=32] {'row'}, dimensions={0} | all-to-all | bytes 3145728 | tf_op jit(solution)/shard_map/all_to_all | solution.py:40
  409.4 24.2 %all_to_all.66 = bf16[8,128,768]{2,1,0:T(8,128)(2,1)S(1)} all-to-all(bf16[8,128,768]{2,1,0:T(8,128)(2,1)S(1)} %broadcast_in_dim.20), channel_id=1, replica_groups=mesh['row'=8,'col'=32] {'row'}, dimensions={0} | all-to-all | bytes 3145728 | tf_op jit(solution)/shard_map/all_to_all | solution.py:33
  433.6 2.6 convolution_convert_fusion
  436.2 5.1 %all-to-all-start.11 = ((bf16[32,32,768]{2,1,0:T(8,128)(2,1)}), bf16[32,32,768]{2,1,0:T(8,128)(2,1)}, u32[]{:S(2)}, u32[]{:S(2)}) async-start(bf16[32,32,768]{2,1,0:T(8,128)(2,1)} %bitcast.26), calls=%async_computation.11 | async-start | bytes 3145728 | tf_op jit(solution)/shard_map/all_to_all | solution.py:40
  442.0 2.5 convolution_convert_fusion.3
  444.5 3.9 convolution_convert_fusion.4
  448.3 2.1 convert_element_type.172
  450.4 1.9 convert_element_type.169
  452.3 28.1 %all-to-all-done.11 = bf16[32,32,768]{2,1,0:T(8,128)(2,1)} async-done(((bf16[32,32,768]{2,1,0:T(8,128)(2,1)}), bf16[32,32,768]{2,1,0:T(8,128)(2,1)}, u32[]{:S(2)}, u32[]{:S(2)}) %all-to-all-start.11) | async-done | bytes 1572896 | tf_op jit(solution)/shard_map/all_to_all | solution.py:40
  480.4 1.6 convert_reduce_fusion
  (77 shorter events, 9.2 us)
Async XLA Ops:
  7.2 226.7 %copy-start = (bf16[6144,256]{1,0:T(8,128)(2,1)S(1)}, bf16[6144,256]{1,0:T(8,128)(2,1)}, u32[]{:S(2)}) copy-start(bf16[6144,256]{1,0:T(8,128)(2,1)} %param.11) | copy-start | bytes 9437188
  8.8 9.8 %all-to-all-start = ((bf16[8,4,768]{2,1,0:T(4,128)(2,1)}), bf16[8,4,768]{2,1,0:T(4,128)(2,1)S(1)}, u32[]{:S(2)}, u32[]{:S(2)}) async-start(bf16[8,4,768]{2,1,0:T(4,128)(2,1)} %reshape_transpose_reshape_broadcast_in_dim.6), calls=%async_computation | async-start | bytes 98304 | tf_op jit(solution)/shard_map/all_to_all | solution.py:65
  21.4 54.0 %all-to-all-start.1 = ((bf16[32,32,768]{2,1,0:T(8,128)(2,1)}), bf16[32,32,768]{2,1,0:T(8,128)(2,1)}, u32[]{:S(2)}, u32[]{:S(2)}) async-start(bf16[32,32,768]{2,1,0:T(8,128)(2,1)} %broadcast_in_dim.14), calls=%async_computation.1 | async-start | bytes 3145728 | tf_op jit(solution)/shard_map/all_to_all | solution.py:33
  32.8 98.1 %all-gather.4.cloned.1.call-start = ((), (), s32[]{:S(2)}) async-start(), calls=%async_computation.16 | async-start | bytes 3244032 | tf_op jit(solution)/shard_map/all_gather | solution.py:104
  103.0 25.4 %copy-start.20 = (bf16[768,768]{1,0:T(8,128)(2,1)S(1)}, bf16[768,768]{1,0:T(8,128)(2,1)}, u32[]{:S(2)}) copy-start(bf16[768,768]{1,0:T(8,128)(2,1)} %param.10) | copy-start | bytes 3538948
  127.2 1.2 copy-start.4
  176.3 0.8 copy-start.14
  189.8 44.0 %all-to-all-start.6 = ((bf16[32,4,6144]{2,1,0:T(4,128)(2,1)}), bf16[32,4,6144]{2,1,0:T(4,128)(2,1)}, u32[]{:S(2)}, u32[]{:S(2)}) async-start(bf16[32,4,6144]{2,1,0:T(4,128)(2,1)} %broadcast_in_dim.18), calls=%async_computation.6 | async-start | bytes 3145728 | tf_op jit(solution)/shard_map/all_to_all | solution.py:124
  194.7 253.6 %reduce-scatter.5.cloned.1.call-start = ((), (), s32[]{:S(2)}) async-start(), calls=%async_computation.15 | async-start | bytes 7077888 | tf_op jit(solution)/shard_map/reduce_scatter | solution.py:183
  196.6 3.7 copy-start.17
  233.9 4.1 copy-start.2
  237.3 0.6 copy-start.13
  243.0 4.6 copy-start.3
  247.0 0.6 copy-start.16
  251.5 82.4 %all-to-all-start.7 = ((bf16[256,8,768]{2,1,0:T(8,128)(2,1)}), bf16[256,8,768]{2,1,0:T(8,128)(2,1)S(1)}, u32[]{:S(2)}, u32[]{:S(2)}) async-start(bf16[256,8,768]{2,1,0:T(8,128)(2,1)} %bitcast.20), calls=%async_computation.7 | async-start | bytes 6291456 | tf_op jit(solution)/shard_map/all_to_all | solution.py:155
  258.6 191.8 %reduce-scatter.3.cloned.1.call-start = ((), (), s32[]{:S(2)}) async-start(), calls=%async_computation.14 | async-start | bytes 7077888 | tf_op jit(solution)/shard_map/reduce_scatter | solution.py:180
  264.1 0.7 copy-start.19
  264.1 0.7 copy-start.18
  334.0 0.9 copy-start.8
  334.9 2.3 copy-start.15
  337.2 0.6 copy-start.9
  338.0 45.0 %copy-start.21 = (bf16[768,768]{1,0:T(8,128)(2,1)S(1)}, bf16[768,768]{1,0:T(8,128)(2,1)}, u32[]{:S(2)}) copy-start(bf16[768,768]{1,0:T(8,128)(2,1)} %param.10) | copy-start | bytes 3538948
  409.4 24.2 %copy-start.22 = (bf16[768,768]{1,0:T(8,128)(2,1)S(1)}, bf16[768,768]{1,0:T(8,128)(2,1)}, u32[]{:S(2)}) copy-start(bf16[768,768]{1,0:T(8,128)(2,1)} %param.9) | copy-start | bytes 3538948
  433.6 2.6 copy-start.6
  436.2 5.1 %copy-start.12 = (f32[8,4,768]{2,1,0:T(4,128)S(1)}, f32[8,4,768]{2,1,0:T(4,128)}, u32[]{:S(2)}) copy-start(f32[8,4,768]{2,1,0:T(4,128)} %get-tuple-element.13) | copy-start | bytes 294916
  436.2 5.2 %copy-start.11 = (bf16[32,768]{1,0:T(8,128)(2,1)S(1)}, bf16[32,768]{1,0:T(8,128)(2,1)}, u32[]{:S(2)}) copy-start(bf16[32,768]{1,0:T(8,128)(2,1)} %add_convert_fusion.3) | copy-start | bytes 147460
  436.2 5.8 %copy-start.5 = (bf16[8,128,768]{2,1,0:T(8,128)(2,1)S(1)}, bf16[8,128,768]{2,1,0:T(8,128)(2,1)}, u32[]{:S(2)}) copy-start(bf16[8,128,768]{2,1,0:T(8,128)(2,1)} %copy-done.4) | copy-start | bytes 4718596
  436.2 44.2 %all-to-all-start.11 = ((bf16[32,32,768]{2,1,0:T(8,128)(2,1)}), bf16[32,32,768]{2,1,0:T(8,128)(2,1)}, u32[]{:S(2)}, u32[]{:S(2)}) async-start(bf16[32,32,768]{2,1,0:T(8,128)(2,1)} %bitcast.26), calls=%async_computation.11 | async-start | bytes 3145728 | tf_op jit(solution)/shard_map/all_to_all | solution.py:40
  442.0 2.5 copy-start.7
  448.3 34.4 %copy-start.1 = (bf16[6144,256]{1,0:T(8,128)(2,1)S(1)}, bf16[6144,256]{1,0:T(8,128)(2,1)}, u32[]{:S(2)}) copy-start(bf16[6144,256]{1,0:T(8,128)(2,1)} %param.11) | copy-start | bytes 9437188
  450.4 31.7 %copy-start.10 = (bf16[32,768]{1,0:T(8,128)(2,1)S(1)}, bf16[32,768]{1,0:T(8,128)(2,1)}, u32[]{:S(2)}) copy-start(bf16[32,768]{1,0:T(8,128)(2,1)} %copy-done.9) | copy-start | bytes 147460
Sparse Core Ops, SparseCore 0:
  36.8 79.9 all-gather.3
  242.2 62.4 reduce-scatter.4
  307.3 50.1 reduce-scatter.2
where the time goes:
time: 491 us; the launch traced here: 489 us
  blocking collectives  196 us (40%)
  waiting for transfers between devices  175 us (36%)
  matrix products  35.1 us (7%)
  starting transfers between devices  33 us (7%)
  local copies, waits for them, and re-layouts  22.5 us (5%)
  between operations  14 us (3%)
  other arithmetic  13.4 us (3%)
    all_to_all x3, blocking collectives, scatter_sum(): got = lax.all_to_all(blocks, axis_name, 0, 0, tiled=True)  93.9 us
    all_to_all x3, blocking collectives, gather_rows(): got = lax.all_to_all(spread, axis_name, 0, 0, tiled=True)  93.3 us
    all_to_all x1, waiting for transfers between devices, on_device(): lax.all_to_all(back_flat.astype(jnp.bfloat16).reshape(col_count, 2 * bloc...  67.2 us
    all_to_all x1, waiting for transfers between devices, gather_rows(): got = lax.all_to_all(spread, axis_name, 0, 0, tiled=True)  41.8 us
    all_to_all x1, waiting for transfers between devices, on_device(): got = lax.all_to_all(payload, 'col', 0, 0, tiled=True)  33.5 us
    all_to_all x1, waiting for transfers between devices, scatter_sum(): got = lax.all_to_all(blocks, axis_name, 0, 0, tiled=True)  28.1 us
    all_to_all x1, starting transfers between devices, gather_rows(): got = lax.all_to_all(spread, axis_name, 0, 0, tiled=True)  11.4 us
  transfers between devices with their start and end apart: 8, of which 5 were waited for; matrix products, arithmetic and copies ran while one was open for 10% of the time, Pallas kernels for 0%

commit v1 on v0

--- a/solution.py
+++ b/solution.py
@@ -6,6 +6,22 @@
 EXPERTS = 4
 gelu_scale = 0.7978845608028654
 gelu_cubic = 0.044715
+
+
+def swapped_with_each(value, axis, split, join):
+    ways, here = (lax.axis_size(axis), lax.axis_index(axis))
+    width = value.shape[split] // ways
+    shape = list(value.shape)
+    shape[split] = width
+    height = shape[join]
+    shape[join] = height * ways
+    full = jnp.zeros(shape, value.dtype)
+    for mask in range(ways):
+        part = lax.dynamic_slice_in_dim(value, (here ^ mask) * width, width, axis=split)
+        if mask:
+            part = lax.ppermute(part, axis, [(d, d ^ mask) for d in range(ways)])
+        full = lax.dynamic_update_slice_in_dim(full, part, (here ^ mask) * height, axis=join)
+    return full
 
 
 def gelu_tanh(value):
@@ -62,7 +78,7 @@
     arrays, tok, width = pair.shape
     block = tok // count
     parts = pair.reshape(arrays, count, block, width).transpose(1, 0, 2, 3)
-    got = lax.all_to_all(parts.reshape(count, arrays * block, width), "row", 0, 0, tiled=True)
+    got = swapped_with_each(parts.reshape(count, arrays * block, width), "row", 0, 0)
     got = got.reshape(count, arrays, block, width).transpose(1, 2, 0, 3)
     return got.reshape(arrays, block, count * width)
 

time: 491 us -> 500 us (1.018)
  starting transfers between devices: 33 us -> 43.4 us
  blocking collectives: 196 us -> 190 us
    ppermute x0 -> x14, starting transfers between devices: none -> 14.5 us  [swapped_with_each(): part = lax.ppermute(part, axis, [(d, d ^ mask) for d in range(ways)])]
    all_to_all x1 -> x0, blocking collectives: 8.78 us -> none  [swap_blocks(): lax.all_to_all(parts.reshape(count, arrays * block, width), 'row', 0, 0,...]
    ppermute x0 -> x14, waiting for transfers between devices: none -> 8.11 us  [swapped_with_each(): part = lax.ppermute(part, axis, [(d, d ^ mask) for d in range(ways)])]
  transfers between devices with their start and end apart: 8 -> 21, of which waited for: 5 -> 7; matrix products, arithmetic and copies ran while one was open for 10% -> 10% of each run, Pallas kernels for 0% -> 0%
where the time goes in v1:
time: 500 us; the launch traced here: 499 us
  blocking collectives  190 us (38%)
  waiting for transfers between devices  178 us (36%)
  starting transfers between devices  43.4 us (9%)
  matrix products  35.1 us (7%)
  local copies, waits for them, and re-layouts  24.4 us (5%)
  between operations  14.4 us (3%)
  other arithmetic  13.4 us (3%)
    all_to_all x3, blocking collectives, scatter_sum(): got = lax.all_to_all(blocks, axis_name, 0, 0, tiled=True)  96.6 us
    all_to_all x3, blocking collectives, gather_rows(): got = lax.all_to_all(spread, axis_name, 0, 0, tiled=True)  93.3 us
    all_to_all x1, waiting for transfers between devices, on_device(): lax.all_to_all(back_flat.astype(jnp.bfloat16).reshape(col_count, 2 * bloc...  67 us
    all_to_all x1, waiting for transfers between devices, gather_rows(): got = lax.all_to_all(spread, axis_name, 0, 0, tiled=True)  40.7 us
    all_to_all x1, waiting for transfers between devices, on_device(): got = lax.all_to_all(payload, 'col', 0, 0, tiled=True)  33.7 us
    all_to_all x1, waiting for transfers between devices, scatter_sum(): got = lax.all_to_all(blocks, axis_name, 0, 0, tiled=True)  28.1 us
    ppermute x14, starting transfers between devices, swapped_with_each(): part = lax.ppermute(part, axis, [(d, d ^ mask) for d in range(ways)])  14.5 us
    all_to_all x1, starting transfers between devices, gather_rows(): got = lax.all_to_all(spread, axis_name, 0, 0, tiled=True)  11.4 us
  transfers between devices with their start and end apart: 21, of which 7 were waited for; matrix products, arithmetic and copies ran while one was open for 10% of the time, Pallas kernels for 0%

profile of v1, /device:TPU:32, one launch (start us, length us, event | category | flops | bytes accessed | tf_op | source)
XLA Modules:
  0.0 498.8 jit_solution(8852873961588842620)
XLA Ops:
  7.2 1.0 reshape_transpose_reshape_broadcast_in_dim.6
  8.3 2.3 collective-permute-start.6
  11.2 1.6 collective-permute-start.4
  12.8 1.7 collective-permute-start.3
  16.0 1.6 collective-permute-start.1
  18.3 1.4 collective-permute-done.1
  21.0 2.2 broadcast_in_dim.14
  23.2 11.4 %all-to-all-start = ((bf16[32,32,768]{2,1,0:T(8,128)(2,1)}), bf16[32,32,768]{2,1,0:T(8,128)(2,1)}, u32[]{:S(2)}, u32[]{:S(2)}) async-start(bf16[32,32,768]{2,1,0:T(8,128)(2,1)} %broadcast_in_dim.14), calls=%async_computation | async-start | bytes 3145728 | tf_op jit(solution)/shard_map/all_to_all | solution.py:49
  35.4 40.7 %all-to-all-done = bf16[32,32,768]{2,1,0:T(8,128)(2,1)} async-done(((bf16[32,32,768]{2,1,0:T(8,128)(2,1)}), bf16[32,32,768]{2,1,0:T(8,128)(2,1)}, u32[]{:S(2)}, u32[]{:S(2)}) %all-to-all-start) | async-done | bytes 1572896 | tf_op jit(solution)/shard_map/all_to_all | solution.py:49
  76.1 3.1 convolution_convert_fusion.2
  79.2 26.5 %all_to_all.50 = bf16[8,128,768]{2,1,0:T(8,128)(2,1)S(1)} all-to-all(bf16[8,128,768]{2,1,0:T(8,128)(2,1)S(1)} %bitcast.112), channel_id=1, replica_groups=mesh['row'=8,'col'=32] {'row'}, dimensions={0} | all-to-all | bytes 3145728 | tf_op jit(solution)/shard_map/all_to_all | solution.py:56
  106.2 24.2 %all_to_all.51 = bf16[8,128,768]{2,1,0:T(8,128)(2,1)S(1)} all-to-all(bf16[8,128,768]{2,1,0:T(8,128)(2,1)S(1)} %broadcast_in_dim.15), channel_id=1, replica_groups=mesh['row'=8,'col'=32] {'row'}, dimensions={0} | all-to-all | bytes 3145728 | tf_op jit(solution)/shard_map/all_to_all | solution.py:49
  130.3 1.2 copy-done.4
  131.5 2.6 fusion.38
  134.1 45.7 %all_to_all.52 = bf16[32,32,768]{2,1,0:T(8,128)(2,1)S(1)} all-to-all(bf16[32,32,768]{2,1,0:T(8,128)(2,1)} %bitcast.111), channel_id=1, replica_groups=mesh['row'=8,'col'=32] {'col'}, dimensions={0} | all-to-all | bytes 3145728 | tf_op jit(solution)/shard_map/all_to_all | solution.py:56
  181.3 1.4 reshape_transpose_reshape_broadcast_in_dim.7
  184.3 1.3 collective-permute-start.13
  185.6 2.1 collective-permute-start.12
  187.7 2.9 collective-permute-start.10
  190.6 3.6 collective-permute-done.8
  194.2 3.0 collective-permute-done.9
  197.4 1.9 broadcast_in_dim.18
  199.3 4.9 all-to-all-start.4
  205.8 3.7 slice.17
  209.6 33.7 %all-to-all-done.4 = bf16[32,4,6144]{2,1,0:T(4,128)(2,1)} async-done(((bf16[32,4,6144]{2,1,0:T(4,128)(2,1)}), bf16[32,4,6144]{2,1,0:T(4,128)(2,1)}, u32[]{:S(2)}, u32[]{:S(2)}) %all-to-all-start.4) | async-done | bytes 1572896 | tf_op jit(solution)/shard_map/all_to_all | solution.py:140
  243.3 3.4 multiply_convert_fusion.8
  247.3 4.1 fusion.4
  251.5 0.9 copy.128
  252.4 4.0 fusion.15
  257.0 1.0 fusion.31
  258.0 1.1 fusion
  259.1 1.9 copy.120
  260.9 7.2 %all-to-all-start.5 = ((bf16[256,8,768]{2,1,0:T(8,128)(2,1)}), bf16[256,8,768]{2,1,0:T(8,128)(2,1)S(1)}, u32[]{:S(2)}, u32[]{:S(2)}) async-start(bf16[256,8,768]{2,1,0:T(8,128)(2,1)} %bitcast.33), calls=%async_computation.5 | async-start | bytes 6291456 | tf_op jit(solution)/shard_map/all_to_all | solution.py:171
  268.4 5.4 %fusion.2 = f32[6144,256]{1,0:T(8,128)} fusion(bf16[32,4,256]{2,0,1:T(8,128)(2,1)} %copy-done.16, bf16[32,4,6144]{2,1,0:T(4,128)(2,1)} %all-to-all-done.4), kind=kOutput, calls=%fused_computation.5 | convolution fusion | flops 405798912 | bytes 7929856 | tf_op jit(solution)/shard_map/dot_general | solution.py:160
  276.5 67.0 %all-to-all-done.5 = bf16[256,8,768]{2,1,0:T(8,128)(2,1)S(1)} async-done(((bf16[256,8,768]{2,1,0:T(8,128)(2,1)}), bf16[256,8,768]{2,1,0:T(8,128)(2,1)S(1)}, u32[]{:S(2)}, u32[]{:S(2)}) %all-to-all-start.5) | async-done | bytes 3145760 | tf_op jit(solution)/shard_map/all_to_all | solution.py:171
  344.4 2.3 slice_reduce_fusion
  347.6 44.9 %all_to_all.53 = bf16[32,32,768]{2,1,0:T(8,128)(2,1)S(1)} all-to-all(bf16[32,32,768]{2,1,0:T(8,128)(2,1)S(1)} %broadcast_in_dim.19), channel_id=1, replica_groups=mesh['row'=8,'col'=32] {'col'}, dimensions={0} | all-to-all | bytes 3145728 | tf_op jit(solution)/shard_map/all_to_all | solution.py:49
  392.5 1.4 convolution_convert_fusion.1
  394.0 24.4 %all_to_all.54 = bf16[8,128,768]{2,1,0:T(8,128)(2,1)S(1)} all-to-all(bf16[8,128,768]{2,1,0:T(8,128)(2,1)S(1)} %bitcast.113), channel_id=1, replica_groups=mesh['row'=8,'col'=32] {'row'}, dimensions={0} | all-to-all | bytes 3145728 | tf_op jit(solution)/shard_map/all_to_all | solution.py:56
  419.0 24.2 %all_to_all.55 = bf16[8,128,768]{2,1,0:T(8,128)(2,1)S(1)} all-to-all(bf16[8,128,768]{2,1,0:T(8,128)(2,1)S(1)} %broadcast_in_dim.20), channel_id=1, replica_groups=mesh['row'=8,'col'=32] {'row'}, dimensions={0} | all-to-all | bytes 3145728 | tf_op jit(solution)/shard_map/all_to_all | solution.py:49
  443.1 2.6 convolution_convert_fusion
  445.8 5.1 %all-to-all-start.9 = ((bf16[32,32,768]{2,1,0:T(8,128)(2,1)}), bf16[32,32,768]{2,1,0:T(8,128)(2,1)}, u32[]{:S(2)}, u32[]{:S(2)}) async-start(bf16[32,32,768]{2,1,0:T(8,128)(2,1)} %bitcast.39), calls=%async_computation.9 | async-start | bytes 3145728 | tf_op jit(solution)/shard_map/all_to_all | solution.py:56
  451.6 2.5 convolution_convert_fusion.3
  454.0 3.9 convolution_convert_fusion.4
  457.9 2.1 convert_element_type.172
  460.0 1.9 convert_element_type.169
  461.9 28.1 %all-to-all-done.9 = bf16[32,32,768]{2,1,0:T(8,128)(2,1)} async-done(((bf16[32,32,768]{2,1,0:T(8,128)(2,1)}), bf16[32,32,768]{2,1,0:T(8,128)(2,1)}, u32[]{:S(2)}, u32[]{:S(2)}) %all-to-all-start.9) | async-done | bytes 1572896 | tf_op jit(solution)/shard_map/all_to_all | solution.py:56
  490.0 1.6 convert_reduce_fusion
  (131 shorter events, 17.8 us)
Async XLA Ops:
  7.2 236.1 %copy-start = (bf16[6144,256]{1,0:T(8,128)(2,1)S(1)}, bf16[6144,256]{1,0:T(8,128)(2,1)}, u32[]{:S(2)}) copy-start(bf16[6144,256]{1,0:T(8,128)(2,1)} %param.11) | copy-start | bytes 9437188
  8.3 7.8 %collective-permute-start.6 = (bf16[1,4,768]{2,1,0:T(4,128)(2,1)S(1)}, bf16[1,4,768]{2,1,0:T(4,128)(2,1)S(1)}, u32[]{:S(2)}, u32[]{:S(2)}) collective-permute-start(bf16[1,4,768]{2,1,0:T(4,128)(2,1)S(1)} %get-tuple-element.21), channel_id=1, source_target_pairs={{0,224},{32,192},{64,160},{96,128},{128,96},{160,64},{192,32},{224... | collective-permute-start | bytes 18440 | tf_op jit(solution)/shard_map/ppermute | solution.py:22
  10.6 7.1 %collective-permute-start.5 = (bf16[1,4,768]{2,1,0:T(4,128)(2,1)S(1)}, bf16[1,4,768]{2,1,0:T(4,128)(2,1)S(1)}, u32[]{:S(2)}, u32[]{:S(2)}) collective-permute-start(bf16[1,4,768]{2,1,0:T(4,128)(2,1)S(1)} %get-tuple-element.22), channel_id=1, source_target_pairs={{0,192},{32,224},{64,128},{96,160},{128,64},{160,96},{192,0},{224,... | collective-permute-start | bytes 18440 | tf_op jit(solution)/shard_map/ppermute | solution.py:22
  11.2 7.0 %collective-permute-start.4 = (bf16[1,4,768]{2,1,0:T(4,128)(2,1)S(1)}, bf16[1,4,768]{2,1,0:T(4,128)(2,1)S(1)}, u32[]{:S(2)}, u32[]{:S(2)}) collective-permute-start(bf16[1,4,768]{2,1,0:T(4,128)(2,1)S(1)} %get-tuple-element.23), channel_id=1, source_target_pairs={{0,160},{32,128},{64,224},{96,192},{128,32},{160,0},{192,96},{224,... | collective-permute-start | bytes 18440 | tf_op jit(solution)/shard_map/ppermute | solution.py:22
  12.8 5.4 %collective-permute-start.3 = (bf16[1,4,768]{2,1,0:T(4,128)(2,1)S(1)}, bf16[1,4,768]{2,1,0:T(4,128)(2,1)S(1)}, u32[]{:S(2)}, u32[]{:S(2)}) collective-permute-start(bf16[1,4,768]{2,1,0:T(4,128)(2,1)S(1)} %get-tuple-element.24), channel_id=1, source_target_pairs={{0,128},{32,160},{64,192},{96,224},{128,0},{160,32},{192,64},{224,... | collective-permute-start | bytes 18440 | tf_op jit(solution)/shard_map/ppermute | solution.py:22
  14.6 3.7 collective-permute-start.2
  16.0 3.6 collective-permute-start.1
  17.7 2.0 collective-permute-start
  23.2 52.9 %all-to-all-start = ((bf16[32,32,768]{2,1,0:T(8,128)(2,1)}), bf16[32,32,768]{2,1,0:T(8,128)(2,1)}, u32[]{:S(2)}, u32[]{:S(2)}) async-start(bf16[32,32,768]{2,1,0:T(8,128)(2,1)} %broadcast_in_dim.14), calls=%async_computation | async-start | bytes 3145728 | tf_op jit(solution)/shard_map/all_to_all | solution.py:49
  34.6 99.5 %all-gather.4.cloned.1.call-start = ((), (), s32[]{:S(2)}) async-start(), calls=%async_computation.14 | async-start | bytes 3244032 | tf_op jit(solution)/shard_map/all_gather | solution.py:120
  106.2 25.4 %copy-start.20 = (bf16[768,768]{1,0:T(8,128)(2,1)S(1)}, bf16[768,768]{1,0:T(8,128)(2,1)}, u32[]{:S(2)}) copy-start(bf16[768,768]{1,0:T(8,128)(2,1)} %param.10) | copy-start | bytes 3538948
  130.3 1.2 copy-start.4
  179.8 0.8 copy-start.14
  183.5 7.0 %collective-permute-start.7 = (bf16[1,4,768]{2,1,0:T(4,128)(2,1)S(1)}, bf16[1,4,768]{2,1,0:T(4,128)(2,1)S(1)}, u32[]{:S(2)}, u32[]{:S(2)}) collective-permute-start(bf16[1,4,768]{2,1,0:T(4,128)(2,1)S(1)} %get-tuple-element.20), channel_id=1, source_target_pairs={{0,32},{32,0},{64,96},{96,64},{128,160},{160,128},{192,224},{224,1... | collective-permute-start | bytes 18440 | tf_op jit(solution)/shard_map/ppermute | solution.py:22
  184.3 13.0 %collective-permute-start.13 = (bf16[1,4,768]{2,1,0:T(4,128)(2,1)S(1)}, bf16[1,4,768]{2,1,0:T(4,128)(2,1)S(1)}, u32[]{:S(2)}, u32[]{:S(2)}) collective-permute-start(bf16[1,4,768]{2,1,0:T(4,128)(2,1)S(1)} %get-tuple-element.14), channel_id=1, source_target_pairs={{0,224},{32,192},{64,160},{96,128},{128,96},{160,64},{192,32},{224... | collective-permute-start | bytes 18440 | tf_op jit(solution)/shard_map/ppermute | solution.py:22
  185.6 11.7 %collective-permute-start.12 = (bf16[1,4,768]{2,1,0:T(4,128)(2,1)S(1)}, bf16[1,4,768]{2,1,0:T(4,128)(2,1)S(1)}, u32[]{:S(2)}, u32[]{:S(2)}) collective-permute-start(bf16[1,4,768]{2,1,0:T(4,128)(2,1)S(1)} %get-tuple-element.15), channel_id=1, source_target_pairs={{0,192},{32,224},{64,128},{96,160},{128,64},{160,96},{192,0},{224,... | collective-permute-start | bytes 18440 | tf_op jit(solution)/shard_map/ppermute | solution.py:22
  187.7 9.6 %collective-permute-start.11 = (bf16[1,4,768]{2,1,0:T(4,128)(2,1)S(1)}, bf16[1,4,768]{2,1,0:T(4,128)(2,1)S(1)}, u32[]{:S(2)}, u32[]{:S(2)}) collective-permute-start(bf16[1,4,768]{2,1,0:T(4,128)(2,1)S(1)} %get-tuple-element.16), channel_id=1, source_target_pairs={{0,160},{32,128},{64,224},{96,192},{128,32},{160,0},{192,96},{224,... | collective-permute-start | bytes 18440 | tf_op jit(solution)/shard_map/ppermute | solution.py:22
  187.7 9.6 %collective-permute-start.10 = (bf16[1,4,768]{2,1,0:T(4,128)(2,1)S(1)}, bf16[1,4,768]{2,1,0:T(4,128)(2,1)S(1)}, u32[]{:S(2)}, u32[]{:S(2)}) collective-permute-start(bf16[1,4,768]{2,1,0:T(4,128)(2,1)S(1)} %get-tuple-element.17), channel_id=1, source_target_pairs={{0,128},{32,160},{64,192},{96,224},{128,0},{160,32},{192,64},{224,... | collective-permute-start | bytes 18440 | tf_op jit(solution)/shard_map/ppermute | solution.py:22
  190.5 3.6 collective-permute-start.8
  194.2 3.1 collective-permute-start.9
  199.3 44.0 %all-to-all-start.4 = ((bf16[32,4,6144]{2,1,0:T(4,128)(2,1)}), bf16[32,4,6144]{2,1,0:T(4,128)(2,1)}, u32[]{:S(2)}, u32[]{:S(2)}) async-start(bf16[32,4,6144]{2,1,0:T(4,128)(2,1)} %broadcast_in_dim.18), calls=%async_computation.4 | async-start | bytes 3145728 | tf_op jit(solution)/shard_map/all_to_all | solution.py:140
  204.2 253.8 %reduce-scatter.5.cloned.1.call-start = ((), (), s32[]{:S(2)}) async-start(), calls=%async_computation.13 | async-start | bytes 7077888 | tf_op jit(solution)/shard_map/reduce_scatter | solution.py:199
  205.8 3.7 copy-start.17
  243.3 4.1 copy-start.2
  246.7 0.6 copy-start.13
  252.4 4.6 copy-start.3
  256.4 0.6 copy-start.16
  260.9 82.6 %all-to-all-start.5 = ((bf16[256,8,768]{2,1,0:T(8,128)(2,1)}), bf16[256,8,768]{2,1,0:T(8,128)(2,1)S(1)}, u32[]{:S(2)}, u32[]{:S(2)}) async-start(bf16[256,8,768]{2,1,0:T(8,128)(2,1)} %bitcast.33), calls=%async_computation.5 | async-start | bytes 6291456 | tf_op jit(solution)/shard_map/all_to_all | solution.py:171
  268.1 191.9 %reduce-scatter.3.cloned.1.call-start = ((), (), s32[]{:S(2)}) async-start(), calls=%async_computation.12 | async-start | bytes 7077888 | tf_op jit(solution)/shard_map/reduce_scatter | solution.py:196
  273.8 0.7 copy-start.19
  273.8 0.7 copy-start.18
  343.5 0.9 copy-start.8
  344.4 2.3 copy-start.15
  346.8 0.6 copy-start.9
  347.6 45.0 %copy-start.21 = (bf16[768,768]{1,0:T(8,128)(2,1)S(1)}, bf16[768,768]{1,0:T(8,128)(2,1)}, u32[]{:S(2)}) copy-start(bf16[768,768]{1,0:T(8,128)(2,1)} %param.10) | copy-start | bytes 3538948
  419.0 24.2 %copy-start.22 = (bf16[768,768]{1,0:T(8,128)(2,1)S(1)}, bf16[768,768]{1,0:T(8,128)(2,1)}, u32[]{:S(2)}) copy-start(bf16[768,768]{1,0:T(8,128)(2,1)} %param.9) | copy-start | bytes 3538948
  443.1 2.6 copy-start.6
  445.8 5.1 %copy-start.12 = (f32[8,4,768]{2,1,0:T(4,128)S(1)}, f32[8,4,768]{2,1,0:T(4,128)}, u32[]{:S(2)}) copy-start(f32[8,4,768]{2,1,0:T(4,128)} %get-tuple-element.13) | copy-start | bytes 294916
  445.8 5.2 %copy-start.11 = (bf16[32,768]{1,0:T(8,128)(2,1)S(1)}, bf16[32,768]{1,0:T(8,128)(2,1)}, u32[]{:S(2)}) copy-start(bf16[32,768]{1,0:T(8,128)(2,1)} %add_convert_fusion.3) | copy-start | bytes 147460
  445.8 5.8 %copy-start.5 = (bf16[8,128,768]{2,1,0:T(8,128)(2,1)S(1)}, bf16[8,128,768]{2,1,0:T(8,128)(2,1)}, u32[]{:S(2)}) copy-start(bf16[8,128,768]{2,1,0:T(8,128)(2,1)} %copy-done.4) | copy-start | bytes 4718596
  445.8 44.2 %all-to-all-start.9 = ((bf16[32,32,768]{2,1,0:T(8,128)(2,1)}), bf16[32,32,768]{2,1,0:T(8,128)(2,1)}, u32[]{:S(2)}, u32[]{:S(2)}) async-start(bf16[32,32,768]{2,1,0:T(8,128)(2,1)} %bitcast.39), calls=%async_computation.9 | async-start | bytes 3145728 | tf_op jit(solution)/shard_map/all_to_all | solution.py:56
  451.6 2.5 copy-start.7
  457.9 34.4 %copy-start.1 = (bf16[6144,256]{1,0:T(8,128)(2,1)S(1)}, bf16[6144,256]{1,0:T(8,128)(2,1)}, u32[]{:S(2)}) copy-start(bf16[6144,256]{1,0:T(8,128)(2,1)} %param.11) | copy-start | bytes 9437188
  460.0 31.7 %copy-start.10 = (bf16[32,768]{1,0:T(8,128)(2,1)S(1)}, bf16[32,768]{1,0:T(8,128)(2,1)}, u32[]{:S(2)}) copy-start(bf16[32,768]{1,0:T(8,128)(2,1)} %copy-done.9) | copy-start | bytes 147460
Sparse Core Ops, SparseCore 0:
  38.6 82.3 all-gather.3
  251.6 62.6 reduce-scatter.4
  316.9 50.1 reduce-scatter.2
